TPU v7x, 512 devices: a whole 4x4x16 slice. The times are simulated.
512 devices in a mesh: sub: 128 (over y, z, core), case: 4 (over x).
Axes of the slice: x: 4, y: 4, z: 16, core: 2. Of those that a mesh axis runs over, the one named last changes fastest.
Arguments:
- load_interior: float32 [128, 128, 4096], P('sub', None, 'case'), may hold values from -6 to 6
- load_boundary: float32 [128, 128, 1024], P('sub', None, 'case'), may hold values from -6 to 6
- cond_blocks: float32 [128, 128, 4096], P('sub', 'case'), may hold values from -0.25 to 0.25
- block_rows: int32 [128, 128], P('sub', 'case'), may hold values from 0 to 15
- block_cols: int32 [128, 128], P('sub', 'case'), may hold values from 0 to 63, as said below
- interface_maps: int32 [128, 7, 2, 1024], P('sub'), may hold values from 0 to 1023, as said below
- merge_maps: float32 [128, 7, 1024, 512], P('sub', None, 'case'), as said below
Outputs:
- leaf_loads: float32 [128, 1024, 128], P('sub', 'case')
- node_loads: float32 [128, 1024, 128], P('sub', 'case')
Inputs may be any that keep to these rules, and one draw needn't show every extreme that they name: `block_cols`: entry k of a substructure's row lies in [(k // 32) * 16, (k // 32 + 1) * 16); blocks may repeat. `interface_maps`: each row of 1024 entries is a permutation; at level index l, slots that agree in all but their lowest l + 1 bits hold equal entries. `merge_maps`: at level index l, slots that agree in all but their lowest l + 1 bits hold equal entries.
All inputs are finite; a program needn't handle non-finite values.
Results may differ from a plain program's by a relative error of at most 0.0003.
Values sent between devices are 32-bit elements; how exact they have to be, the bound alone decides.
No kernel may reach another device: no remote copies, remote signals or barrier semaphores. Data moves between devices by JAX's collectives and lax.ppermute only.
A program may use at most 64 MiB of HBM per device.

v0:
```python
import jax
import jax.numpy as jnp
from jax import lax
from jax.sharding import PartitionSpec as P

BLK = 64


def from_partner(value, axis, distance):
    mask = 2**distance
    pairs = [(source, source ^ mask) for source in range(lax.axis_size(axis))]
    return lax.ppermute(value, axis, pairs)


def on_device(
    load_interior, load_boundary, cond_blocks, block_rows, block_cols, interface_maps, merge_maps
):
    interior, boundary = (
        lax.all_to_all(load_interior, "sub", split_axis=1, concat_axis=0, tiled=True),
        lax.all_to_all(load_boundary, "sub", split_axis=1, concat_axis=0, tiled=True),
    )
    interior = jnp.transpose(interior[:, 0, :])
    boundary = jnp.transpose(boundary[:, 0, :])
    local_rows = interior.shape[0]
    num_cases = interior.shape[1]
    block_count = cond_blocks.shape[1]
    block_size = BLK
    blocks = cond_blocks[0].reshape(block_count, block_size, block_size)
    quarter = boundary.shape[0]
    groups = lax.axis_size("case")
    full_rows = quarter * groups
    position = lax.axis_index("case")
    local_cols = block_cols[0] - position * (local_rows // block_size)
    pieces = jnp.take(
        interior.reshape(local_rows // block_size, block_size, num_cases), local_cols, axis=0
    )
    products = jnp.einsum("krc,kcn->krn", blocks, pieces, precision=lax.Precision.HIGHEST)
    row_blocks = full_rows // block_size
    onehot = (block_rows[0][None, :] == jnp.arange(row_blocks, dtype=jnp.int32)[:, None]).astype(
        jnp.float32
    )
    partial_value = jnp.dot(
        onehot,
        products.reshape(block_count, block_size * num_cases),
        precision=lax.Precision.HIGHEST,
    )
    partial_value = partial_value.reshape(full_rows, num_cases)
    embedded = lax.dynamic_update_slice(
        jnp.zeros((full_rows, num_cases), jnp.float32), boundary, (position * quarter, 0)
    )
    contribution = embedded - partial_value
    current = lax.psum(contribution, "case")
    leaf_share = lax.dynamic_slice_in_dim(current, position * quarter, quarter, 0)
    slot = lax.axis_index("sub")
    levels = lax.axis_size("sub").bit_length() - 1
    nodes = jnp.zeros((quarter, num_cases), jnp.float32)
    for level in range(1, levels + 1):
        half = 1 << level - 1
        maps = interface_maps[0, level - 1]
        matrix = merge_maps[0, level - 1]
        shared_rows = matrix.shape[1]
        kept_index = jnp.concatenate([maps[0, shared_rows:], maps[1, shared_rows:] + full_rows])
        mine = lax.dynamic_slice_in_dim(kept_index, position * quarter, quarter)
        other = from_partner(current, "sub", level - 1)
        own_full, other_full = (current, other)
        upper = slot // half % 2 == 1
        left_full = jnp.where(upper, other_full, own_full)
        right_full = jnp.where(upper, own_full, other_full)
        stacked = jnp.concatenate([left_full, right_full], axis=0)
        shared = jnp.take(stacked, maps[0, :shared_rows], axis=0) + jnp.take(
            stacked, maps[1, :shared_rows] + full_rows, axis=0
        )
        parent = jnp.take(stacked, mine, axis=0) - jnp.dot(
            matrix, shared, precision=lax.Precision.HIGHEST
        )
        is_node = slot % (2 * half) == half
        if level == levels:
            is_node = jnp.logical_or(is_node, slot == 0)
        nodes = jnp.where(is_node, parent, nodes)
        if level < levels:
            current = lax.all_gather(parent, "case", axis=0, tiled=True)
    return (leaf_share[None], nodes[None])


def solution(mesh):
    placed = (
        P("sub", None, "case"),
        P("sub", None, "case"),
        P("sub", "case", None),
        P("sub", "case"),
        P("sub", "case"),
        P("sub", None, None, None),
        P("sub", None, "case", None),
    )
    return jax.shard_map(
        on_device,
        mesh=mesh,
        in_specs=placed,
        out_specs=(P("sub", "case", None), P("sub", "case", None)),
        check_vma=False,
    )
```

profile of v0, /device:TPU:8, one launch (start us, length us, event | category | flops | bytes accessed | tf_op | source)
XLA Modules:
  0.0 423.4 jit_solution(13161478264808261519)
XLA Ops:
  8.9 19.6 %all-to-all-start = ((f32[1,128,256]{2,0,1:T(1,128)}), f32[1,128,256]{2,0,1:T(1,128)S(1)}, u32[]{:S(2)}, u32[]{:S(2)}) async-start(f32[1,128,256]{2,0,1:T(1,128)} %copy.64), calls=%async_computation | async-start | bytes 262144 | tf_op jit(solution)/shard_map/all_to_all | solution.py:20
  28.5 2.4 copy.66
  32.8 12.9 %all-to-all-done = f32[1,128,256]{2,0,1:T(1,128)S(1)} async-done(((f32[1,128,256]{2,0,1:T(1,128)}), f32[1,128,256]{2,0,1:T(1,128)S(1)}, u32[]{:S(2)}, u32[]{:S(2)}) %all-to-all-start) | async-done | bytes 131104 | tf_op jit(solution)/shard_map/all_to_all | solution.py:20
  45.7 7.2 %all-to-all-start.1 = ((f32[1,128,1024]{2,0,1:T(1,128)}), f32[1,128,1024]{2,0,1:T(1,128)S(1)}, u32[]{:S(2)}, u32[]{:S(2)}) async-start(f32[1,128,1024]{2,0,1:T(1,128)} %copy.66), calls=%async_computation.1 | async-start | bytes 1048576 | tf_op jit(solution)/shard_map/all_to_all | solution.py:19
  55.1 31.4 %all-to-all-done.1 = f32[1,128,1024]{2,0,1:T(1,128)S(1)} async-done(((f32[1,128,1024]{2,0,1:T(1,128)}), f32[1,128,1024]{2,0,1:T(1,128)S(1)}, u32[]{:S(2)}, u32[]{:S(2)}) %all-to-all-start.1) | async-done | bytes 524320 | tf_op jit(solution)/shard_map/all_to_all | solution.py:19
  90.9 50.0 %all-reduce.2.cloned.1.call-done = f32[1024,128]{1,0:T(8,128)} async-done(((f32[1024,128]{1,0:T(8,128)}), f32[1024,128]{1,0:T(8,128)}) %all-reduce.2.cloned.1.call-update) | async-done | bytes 524304 | tf_op jit(solution)/shard_map/psum | solution.py:52
  150.9 12.8 %all_gather.18 = f32[1024,128]{0,1:T(8,128)S(1)} all-gather(f32[256,128]{0,1:T(8,128)S(1)} %fusion.8), channel_id=1, replica_groups=mesh['sub'=128,'case'=4] {'case'}, dimensions={0}, use_global_device_ids=true | all-gather | bytes 655360 | tf_op jit(solution)/shard_map/all_gather | solution.py:81
  163.6 3.6 collective-permute-start.1
  167.4 9.3 %collective-permute-done.1 = f32[1024,128]{0,1:T(8,128)S(1)} collective-permute-done((f32[1024,128]{0,1:T(8,128)S(1)}, f32[1024,128]{0,1:T(8,128)S(1)}, u32[]{:S(2)}, u32[]{:S(2)}) %collective-permute-start.1) | collective-permute-done | bytes 524320 | tf_op jit(solution)/shard_map/ppermute | solution.py:12
  182.0 13.1 %all_gather.19 = f32[1024,128]{0,1:T(8,128)S(1)} all-gather(f32[256,128]{0,1:T(8,128)S(1)} %fusion.7), channel_id=1, replica_groups=mesh['sub'=128,'case'=4] {'case'}, dimensions={0}, use_global_device_ids=true | all-gather | bytes 655360 | tf_op jit(solution)/shard_map/all_gather | solution.py:81
  195.1 4.4 %collective-permute-start.2 = (f32[1024,128]{0,1:T(8,128)S(1)}, f32[1024,128]{0,1:T(8,128)S(1)}, u32[]{:S(2)}, u32[]{:S(2)}) collective-permute-start(f32[1024,128]{0,1:T(8,128)S(1)} %all_gather.19), channel_id=1, source_target_pairs={{0,16},{4,20},{8,24},{12,28},{16,0},{20,4},{24,8},{28,12},{32,48},... | collective-permute-start | bytes 1572872 | tf_op jit(solution)/shard_map/ppermute | solution.py:12
  199.6 16.8 %collective-permute-done.2 = f32[1024,128]{0,1:T(8,128)S(1)} collective-permute-done((f32[1024,128]{0,1:T(8,128)S(1)}, f32[1024,128]{0,1:T(8,128)S(1)}, u32[]{:S(2)}, u32[]{:S(2)}) %collective-permute-start.2) | collective-permute-done | bytes 524320 | tf_op jit(solution)/shard_map/ppermute | solution.py:12
  221.8 13.3 %all_gather.20 = f32[1024,128]{0,1:T(8,128)S(1)} all-gather(f32[256,128]{0,1:T(8,128)S(1)} %fusion.6), channel_id=1, replica_groups=mesh['sub'=128,'case'=4] {'case'}, dimensions={0}, use_global_device_ids=true | all-gather | bytes 655360 | tf_op jit(solution)/shard_map/all_gather | solution.py:81
  235.1 7.6 %collective-permute-start.3 = (f32[1024,128]{0,1:T(8,128)S(1)}, f32[1024,128]{0,1:T(8,128)S(1)}, u32[]{:S(2)}, u32[]{:S(2)}) collective-permute-start(f32[1024,128]{0,1:T(8,128)S(1)} %all_gather.20), channel_id=1, source_target_pairs={{0,32},{4,36},{8,40},{12,44},{16,48},{20,52},{24,56},{28,60},{32,0... | collective-permute-start | bytes 1572872 | tf_op jit(solution)/shard_map/ppermute | solution.py:12
  242.8 40.0 %collective-permute-done.3 = f32[1024,128]{0,1:T(8,128)S(1)} collective-permute-done((f32[1024,128]{0,1:T(8,128)S(1)}, f32[1024,128]{0,1:T(8,128)S(1)}, u32[]{:S(2)}, u32[]{:S(2)}) %collective-permute-start.3) | collective-permute-done | bytes 524320 | tf_op jit(solution)/shard_map/ppermute | solution.py:12
  288.1 12.8 %all_gather.21 = f32[1024,128]{0,1:T(8,128)S(1)} all-gather(f32[256,128]{0,1:T(8,128)S(1)} %fusion.5), channel_id=1, replica_groups=mesh['sub'=128,'case'=4] {'case'}, dimensions={0}, use_global_device_ids=true | all-gather | bytes 655360 | tf_op jit(solution)/shard_map/all_gather | solution.py:81
  300.9 11.2 %collective-permute-start.4 = (f32[1024,128]{0,1:T(8,128)S(1)}, f32[1024,128]{0,1:T(8,128)S(1)}, u32[]{:S(2)}, u32[]{:S(2)}) collective-permute-start(f32[1024,128]{0,1:T(8,128)S(1)} %all_gather.21), channel_id=1, source_target_pairs={{0,64},{4,68},{8,72},{12,76},{16,80},{20,84},{24,88},{28,92},{32,9... | collective-permute-start | bytes 1572872 | tf_op jit(solution)/shard_map/ppermute | solution.py:12
  312.1 36.2 %collective-permute-done.4 = f32[1024,128]{0,1:T(8,128)S(1)} collective-permute-done((f32[1024,128]{0,1:T(8,128)S(1)}, f32[1024,128]{0,1:T(8,128)S(1)}, u32[]{:S(2)}, u32[]{:S(2)}) %collective-permute-start.4) | collective-permute-done | bytes 524320 | tf_op jit(solution)/shard_map/ppermute | solution.py:12
  353.6 13.2 %all_gather.22 = f32[1024,128]{0,1:T(8,128)S(1)} all-gather(f32[256,128]{0,1:T(8,128)S(1)} %fusion.4), channel_id=1, replica_groups=mesh['sub'=128,'case'=4] {'case'}, dimensions={0}, use_global_device_ids=true | all-gather | bytes 655360 | tf_op jit(solution)/shard_map/all_gather | solution.py:81
  366.8 2.4 collective-permute-start.5
  369.3 10.0 %collective-permute-done.5 = f32[1024,128]{0,1:T(8,128)S(1)} collective-permute-done((f32[1024,128]{0,1:T(8,128)S(1)}, f32[1024,128]{0,1:T(8,128)S(1)}, u32[]{:S(2)}, u32[]{:S(2)}) %collective-permute-start.5) | collective-permute-done | bytes 524320 | tf_op jit(solution)/shard_map/ppermute | solution.py:12
  384.6 13.3 %all_gather.23 = f32[1024,128]{0,1:T(8,128)S(1)} all-gather(f32[256,128]{0,1:T(8,128)S(1)} %fusion.3), channel_id=1, replica_groups=mesh['sub'=128,'case'=4] {'case'}, dimensions={0}, use_global_device_ids=true | all-gather | bytes 655360 | tf_op jit(solution)/shard_map/all_gather | solution.py:81
  397.8 4.0 collective-permute-start.6
  403.5 6.9 %collective-permute-done.6 = f32[1024,128]{0,1:T(8,128)S(1)} collective-permute-done((f32[1024,128]{0,1:T(8,128)S(1)}, f32[1024,128]{0,1:T(8,128)S(1)}, u32[]{:S(2)}, u32[]{:S(2)}) %collective-permute-start.6) | collective-permute-done | bytes 524320 | tf_op jit(solution)/shard_map/ppermute | solution.py:12
  (140 shorter events, 53.6 us)
Async XLA Ops:
  7.2 47.8 %copy-start.1 = (s32[1,32]{1,0:T(1,128)S(1)}, s32[1,32]{1,0:T(1,128)}, u32[]{:S(2)}) copy-start(s32[1,32]{1,0:T(1,128)} %param.15) | copy-start | bytes 388
  8.9 36.8 %all-to-all-start = ((f32[1,128,256]{2,0,1:T(1,128)}), f32[1,128,256]{2,0,1:T(1,128)S(1)}, u32[]{:S(2)}, u32[]{:S(2)}) async-start(f32[1,128,256]{2,0,1:T(1,128)} %copy.64), calls=%async_computation | async-start | bytes 262144 | tf_op jit(solution)/shard_map/all_to_all | solution.py:20
  45.7 40.8 %all-to-all-start.1 = ((f32[1,128,1024]{2,0,1:T(1,128)}), f32[1,128,1024]{2,0,1:T(1,128)S(1)}, u32[]{:S(2)}, u32[]{:S(2)}) async-start(f32[1,128,1024]{2,0,1:T(1,128)} %copy.66), calls=%async_computation.1 | async-start | bytes 1048576 | tf_op jit(solution)/shard_map/all_to_all | solution.py:19
  52.9 87.9 %all-reduce.2.cloned.1.call-start = ((), (), s32[]{:S(2)}) async-start(), calls=%async_computation.2 | async-start | bytes 1048576 | tf_op jit(solution)/shard_map/psum | solution.py:52
  54.9 33.8 %copy-start = (s32[1,32]{1,0:T(1,128)S(1)}, s32[1,32]{1,0:T(1,128)}, u32[]{:S(2)}) copy-start(s32[1,32]{1,0:T(1,128)} %param.14) | copy-start | bytes 388
  140.8 4.0 collective-permute-start
  163.6 13.0 %collective-permute-start.1 = (f32[1024,128]{0,1:T(8,128)S(1)}, f32[1024,128]{0,1:T(8,128)S(1)}, u32[]{:S(2)}, u32[]{:S(2)}) collective-permute-start(f32[1024,128]{0,1:T(8,128)S(1)} %all_gather.18), channel_id=1, source_target_pairs={{0,8},{4,12},{8,0},{12,4},{16,24},{20,28},{24,16},{28,20},{32,40},... | collective-permute-start | bytes 1572872 | tf_op jit(solution)/shard_map/ppermute | solution.py:12
  195.1 21.3 %collective-permute-start.2 = (f32[1024,128]{0,1:T(8,128)S(1)}, f32[1024,128]{0,1:T(8,128)S(1)}, u32[]{:S(2)}, u32[]{:S(2)}) collective-permute-start(f32[1024,128]{0,1:T(8,128)S(1)} %all_gather.19), channel_id=1, source_target_pairs={{0,16},{4,20},{8,24},{12,28},{16,0},{20,4},{24,8},{28,12},{32,48},... | collective-permute-start | bytes 1572872 | tf_op jit(solution)/shard_map/ppermute | solution.py:12
  235.1 47.6 %collective-permute-start.3 = (f32[1024,128]{0,1:T(8,128)S(1)}, f32[1024,128]{0,1:T(8,128)S(1)}, u32[]{:S(2)}, u32[]{:S(2)}) collective-permute-start(f32[1024,128]{0,1:T(8,128)S(1)} %all_gather.20), channel_id=1, source_target_pairs={{0,32},{4,36},{8,40},{12,44},{16,48},{20,52},{24,56},{28,60},{32,0... | collective-permute-start | bytes 1572872 | tf_op jit(solution)/shard_map/ppermute | solution.py:12
  300.9 47.4 %collective-permute-start.4 = (f32[1024,128]{0,1:T(8,128)S(1)}, f32[1024,128]{0,1:T(8,128)S(1)}, u32[]{:S(2)}, u32[]{:S(2)}) collective-permute-start(f32[1024,128]{0,1:T(8,128)S(1)} %all_gather.21), channel_id=1, source_target_pairs={{0,64},{4,68},{8,72},{12,76},{16,80},{20,84},{24,88},{28,92},{32,9... | collective-permute-start | bytes 1572872 | tf_op jit(solution)/shard_map/ppermute | solution.py:12
  366.8 12.5 %collective-permute-start.5 = (f32[1024,128]{0,1:T(8,128)S(1)}, f32[1024,128]{0,1:T(8,128)S(1)}, u32[]{:S(2)}, u32[]{:S(2)}) collective-permute-start(f32[1024,128]{0,1:T(8,128)S(1)} %all_gather.22), channel_id=1, source_target_pairs={{0,128},{4,132},{8,136},{12,140},{16,144},{20,148},{24,152},{28,15... | collective-permute-start | bytes 1572872 | tf_op jit(solution)/shard_map/ppermute | solution.py:12
  397.8 12.6 %collective-permute-start.6 = (f32[1024,128]{0,1:T(8,128)S(1)}, f32[1024,128]{0,1:T(8,128)S(1)}, u32[]{:S(2)}, u32[]{:S(2)}) collective-permute-start(f32[1024,128]{0,1:T(8,128)S(1)} %all_gather.23), channel_id=1, source_target_pairs={{0,256},{4,260},{8,264},{12,268},{16,272},{20,276},{24,280},{28,28... | collective-permute-start | bytes 1572872 | tf_op jit(solution)/shard_map/ppermute | solution.py:12
Sparse Core Ops, SparseCore 0:
  91.0 49.8 all-reduce.1
where the time goes:
time: 424 us; the launch traced here: 423 us
  waiting for transfers between devices  215 us (51%)
  blocking collectives  78.5 us (19%)
  starting transfers between devices  62.1 us (15%)
  local copies, waits for them, and re-layouts  32.1 us (8%)
  matrix products  15.4 us (4%)
  between operations  15.3 us (4%)
  other arithmetic  4.42 us (1%)
    ppermute x7, waiting for transfers between devices, from_partner(): return lax.ppermute(value, axis, pairs)  121 us
    all_gather x6, blocking collectives, on_device(): current = lax.all_gather(parent, 'case', axis=0, tiled=True)  78.5 us
    psum x1, waiting for transfers between devices, on_device(): current = lax.psum(contribution, 'case')  50 us
    ppermute x7, starting transfers between devices, from_partner(): return lax.ppermute(value, axis, pairs)  35.3 us
    all_to_all x1, waiting for transfers between devices, on_device(): lax.all_to_all(load_interior, 'sub', split_axis=1, concat_axis=0, tiled=T...  31.4 us
    all_to_all x1, starting transfers between devices, on_device(): lax.all_to_all(load_boundary, 'sub', split_axis=1, concat_axis=0, tiled=T...  19.6 us
    dot_general x7, matrix products, on_device(): jnp.dot(matrix, shared, precision=lax.Precision.HIGHEST)  13.2 us
    all_to_all x1, waiting for transfers between devices, on_device(): lax.all_to_all(load_boundary, 'sub', split_axis=1, concat_axis=0, tiled=T...  12.9 us
  transfers between devices with their start and end apart: 10, of which 10 were waited for; matrix products, arithmetic and copies ran while one was open for 2% of the time, Pallas kernels for 0%

commit v1 on v0

--- a/solution.py
+++ b/solution.py
@@ -49,7 +49,7 @@
         jnp.zeros((full_rows, num_cases), jnp.float32), boundary, (position * quarter, 0)
     )
     contribution = embedded - partial_value
-    current = lax.psum(contribution, "case")
+    current = jnp.sum(lax.all_gather(contribution, "case"), axis=0)
     leaf_share = lax.dynamic_slice_in_dim(current, position * quarter, quarter, 0)
     slot = lax.axis_index("sub")
     levels = lax.axis_size("sub").bit_length() - 1

time: 424 us -> 406 us (0.958)
  waiting for transfers between devices: 215 us -> 197 us
    psum x1 -> x0, waiting for transfers between devices: 50 us -> none  [on_device(): current = lax.psum(contribution, 'case')]
    all_gather x0 -> x1, waiting for transfers between devices: none -> 29.7 us  [on_device(): current = jnp.sum(lax.all_gather(contribution, 'case'), axis=0)]
where the time goes in v1:
time: 406 us; the launch traced here: 405 us
  waiting for transfers between devices  197 us (49%)
  blocking collectives  79.8 us (20%)
  starting transfers between devices  62 us (15%)
  local copies, waits for them, and re-layouts  31.2 us (8%)
  matrix products  15.4 us (4%)
  between operations  15.3 us (4%)
  other arithmetic  4.47 us (1%)
    ppermute x7, waiting for transfers between devices, from_partner(): return lax.ppermute(value, axis, pairs)  121 us
    all_gather x6, blocking collectives, on_device(): current = lax.all_gather(parent, 'case', axis=0, tiled=True)  79.8 us
    ppermute x7, starting transfers between devices, from_partner(): return lax.ppermute(value, axis, pairs)  35.2 us
    all_to_all x1, waiting for transfers between devices, on_device(): lax.all_to_all(load_interior, 'sub', split_axis=1, concat_axis=0, tiled=T...  31.6 us
    all_gather x1, waiting for transfers between devices, on_device(): current = jnp.sum(lax.all_gather(contribution, 'case'), axis=0)  29.7 us
    all_to_all x1, starting transfers between devices, on_device(): lax.all_to_all(load_boundary, 'sub', split_axis=1, concat_axis=0, tiled=T...  19.6 us
    all_to_all x1, waiting for transfers between devices, on_device(): lax.all_to_all(load_boundary, 'sub', split_axis=1, concat_axis=0, tiled=T...  13.8 us
    dot_general x7, matrix products, on_device(): jnp.dot(matrix, shared, precision=lax.Precision.HIGHEST)  13.2 us
  transfers between devices with their start and end apart: 10, of which 10 were waited for; matrix products, arithmetic and copies ran while one was open for 2% of the time, Pallas kernels for 0%

profile of v1, /device:TPU:8, one launch (start us, length us, event | category | flops | bytes accessed | tf_op | source)
XLA Modules:
  0.0 404.8 jit_solution(2131480566072497121)
XLA Ops:
  8.9 19.6 %all-to-all-start = ((f32[1,128,256]{2,0,1:T(1,128)}), f32[1,128,256]{2,0,1:T(1,128)S(1)}, u32[]{:S(2)}, u32[]{:S(2)}) async-start(f32[1,128,256]{2,0,1:T(1,128)} %copy.94), calls=%async_computation | async-start | bytes 262144 | tf_op jit(solution)/shard_map/all_to_all | solution.py:20
  28.5 2.4 copy.96
  31.9 13.8 %all-to-all-done = f32[1,128,256]{2,0,1:T(1,128)S(1)} async-done(((f32[1,128,256]{2,0,1:T(1,128)}), f32[1,128,256]{2,0,1:T(1,128)S(1)}, u32[]{:S(2)}, u32[]{:S(2)}) %all-to-all-start) | async-done | bytes 131104 | tf_op jit(solution)/shard_map/all_to_all | solution.py:20
  45.7 7.2 %all-to-all-start.1 = ((f32[1,128,1024]{2,0,1:T(1,128)}), f32[1,128,1024]{2,0,1:T(1,128)S(1)}, u32[]{:S(2)}, u32[]{:S(2)}) async-start(f32[1,128,1024]{2,0,1:T(1,128)} %copy.96), calls=%async_computation.1 | async-start | bytes 1048576 | tf_op jit(solution)/shard_map/all_to_all | solution.py:19
  54.9 31.6 %all-to-all-done.1 = f32[1,128,1024]{2,0,1:T(1,128)S(1)} async-done(((f32[1,128,1024]{2,0,1:T(1,128)}), f32[1,128,1024]{2,0,1:T(1,128)S(1)}, u32[]{:S(2)}, u32[]{:S(2)}) %all-to-all-start.1) | async-done | bytes 524320 | tf_op jit(solution)/shard_map/all_to_all | solution.py:19
  91.3 29.7 %all-gather.3.cloned.1.call-done = f32[4096,128]{1,0:T(8,128)} async-done(((f32[1024,128]{1,0:T(8,128)}), f32[4096,128]{1,0:T(8,128)}) %all-gather.3.cloned.1.call-update) | async-done | bytes 2097168 | tf_op jit(solution)/shard_map/all_gather | solution.py:52
  131.5 13.5 %all_gather.26 = f32[1024,128]{0,1:T(8,128)S(1)} all-gather(f32[256,128]{0,1:T(8,128)S(1)} %fusion.8), channel_id=1, replica_groups=mesh['sub'=128,'case'=4] {'case'}, dimensions={0}, use_global_device_ids=true | all-gather | bytes 655360 | tf_op jit(solution)/shard_map/all_gather | solution.py:81
  145.0 3.6 collective-permute-start.1
  148.8 8.5 %collective-permute-done.1 = f32[1024,128]{0,1:T(8,128)S(1)} collective-permute-done((f32[1024,128]{0,1:T(8,128)S(1)}, f32[1024,128]{0,1:T(8,128)S(1)}, u32[]{:S(2)}, u32[]{:S(2)}) %collective-permute-start.1) | collective-permute-done | bytes 524320 | tf_op jit(solution)/shard_map/ppermute | solution.py:12
  162.6 13.3 %all_gather.27 = f32[1024,128]{0,1:T(8,128)S(1)} all-gather(f32[256,128]{0,1:T(8,128)S(1)} %fusion.7), channel_id=1, replica_groups=mesh['sub'=128,'case'=4] {'case'}, dimensions={0}, use_global_device_ids=true | all-gather | bytes 655360 | tf_op jit(solution)/shard_map/all_gather | solution.py:81
  175.9 4.4 %collective-permute-start.2 = (f32[1024,128]{0,1:T(8,128)S(1)}, f32[1024,128]{0,1:T(8,128)S(1)}, u32[]{:S(2)}, u32[]{:S(2)}) collective-permute-start(f32[1024,128]{0,1:T(8,128)S(1)} %all_gather.27), channel_id=1, source_target_pairs={{0,16},{4,20},{8,24},{12,28},{16,0},{20,4},{24,8},{28,12},{32,48},... | collective-permute-start | bytes 1572872 | tf_op jit(solution)/shard_map/ppermute | solution.py:12
  180.4 16.8 %collective-permute-done.2 = f32[1024,128]{0,1:T(8,128)S(1)} collective-permute-done((f32[1024,128]{0,1:T(8,128)S(1)}, f32[1024,128]{0,1:T(8,128)S(1)}, u32[]{:S(2)}, u32[]{:S(2)}) %collective-permute-start.2) | collective-permute-done | bytes 524320 | tf_op jit(solution)/shard_map/ppermute | solution.py:12
  202.5 13.3 %all_gather.28 = f32[1024,128]{0,1:T(8,128)S(1)} all-gather(f32[256,128]{0,1:T(8,128)S(1)} %fusion.6), channel_id=1, replica_groups=mesh['sub'=128,'case'=4] {'case'}, dimensions={0}, use_global_device_ids=true | all-gather | bytes 655360 | tf_op jit(solution)/shard_map/all_gather | solution.py:81
  215.8 7.7 %collective-permute-start.3 = (f32[1024,128]{0,1:T(8,128)S(1)}, f32[1024,128]{0,1:T(8,128)S(1)}, u32[]{:S(2)}, u32[]{:S(2)}) collective-permute-start(f32[1024,128]{0,1:T(8,128)S(1)} %all_gather.28), channel_id=1, source_target_pairs={{0,32},{4,36},{8,40},{12,44},{16,48},{20,52},{24,56},{28,60},{32,0... | collective-permute-start | bytes 1572872 | tf_op jit(solution)/shard_map/ppermute | solution.py:12
  223.5 39.6 %collective-permute-done.3 = f32[1024,128]{0,1:T(8,128)S(1)} collective-permute-done((f32[1024,128]{0,1:T(8,128)S(1)}, f32[1024,128]{0,1:T(8,128)S(1)}, u32[]{:S(2)}, u32[]{:S(2)}) %collective-permute-start.3) | collective-permute-done | bytes 524320 | tf_op jit(solution)/shard_map/ppermute | solution.py:12
  268.5 13.3 %all_gather.29 = f32[1024,128]{0,1:T(8,128)S(1)} all-gather(f32[256,128]{0,1:T(8,128)S(1)} %fusion.5), channel_id=1, replica_groups=mesh['sub'=128,'case'=4] {'case'}, dimensions={0}, use_global_device_ids=true | all-gather | bytes 655360 | tf_op jit(solution)/shard_map/all_gather | solution.py:81
  281.8 11.1 %collective-permute-start.4 = (f32[1024,128]{0,1:T(8,128)S(1)}, f32[1024,128]{0,1:T(8,128)S(1)}, u32[]{:S(2)}, u32[]{:S(2)}) collective-permute-start(f32[1024,128]{0,1:T(8,128)S(1)} %all_gather.29), channel_id=1, source_target_pairs={{0,64},{4,68},{8,72},{12,76},{16,80},{20,84},{24,88},{28,92},{32,9... | collective-permute-start | bytes 1572872 | tf_op jit(solution)/shard_map/ppermute | solution.py:12
  292.9 36.6 %collective-permute-done.4 = f32[1024,128]{0,1:T(8,128)S(1)} collective-permute-done((f32[1024,128]{0,1:T(8,128)S(1)}, f32[1024,128]{0,1:T(8,128)S(1)}, u32[]{:S(2)}, u32[]{:S(2)}) %collective-permute-start.4) | collective-permute-done | bytes 524320 | tf_op jit(solution)/shard_map/ppermute | solution.py:12
  334.8 13.0 %all_gather.30 = f32[1024,128]{0,1:T(8,128)S(1)} all-gather(f32[256,128]{0,1:T(8,128)S(1)} %fusion.4), channel_id=1, replica_groups=mesh['sub'=128,'case'=4] {'case'}, dimensions={0}, use_global_device_ids=true | all-gather | bytes 655360 | tf_op jit(solution)/shard_map/all_gather | solution.py:81
  347.8 2.4 collective-permute-start.5
  350.2 10.2 %collective-permute-done.5 = f32[1024,128]{0,1:T(8,128)S(1)} collective-permute-done((f32[1024,128]{0,1:T(8,128)S(1)}, f32[1024,128]{0,1:T(8,128)S(1)}, u32[]{:S(2)}, u32[]{:S(2)}) %collective-permute-start.5) | collective-permute-done | bytes 524320 | tf_op jit(solution)/shard_map/ppermute | solution.py:12
  365.8 13.4 %all_gather.31 = f32[1024,128]{0,1:T(8,128)S(1)} all-gather(f32[256,128]{0,1:T(8,128)S(1)} %fusion.3), channel_id=1, replica_groups=mesh['sub'=128,'case'=4] {'case'}, dimensions={0}, use_global_device_ids=true | all-gather | bytes 655360 | tf_op jit(solution)/shard_map/all_gather | solution.py:81
  379.3 4.0 collective-permute-start.6
  384.0 7.9 %collective-permute-done.6 = f32[1024,128]{0,1:T(8,128)S(1)} collective-permute-done((f32[1024,128]{0,1:T(8,128)S(1)}, f32[1024,128]{0,1:T(8,128)S(1)}, u32[]{:S(2)}, u32[]{:S(2)}) %collective-permute-start.6) | collective-permute-done | bytes 524320 | tf_op jit(solution)/shard_map/ppermute | solution.py:12
  (141 shorter events, 52.6 us)
Async XLA Ops:
  7.2 47.5 %copy-start.1 = (s32[1,32]{1,0:T(1,128)S(1)}, s32[1,32]{1,0:T(1,128)}, u32[]{:S(2)}) copy-start(s32[1,32]{1,0:T(1,128)} %param.15) | copy-start | bytes 388
  8.9 36.8 %all-to-all-start = ((f32[1,128,256]{2,0,1:T(1,128)}), f32[1,128,256]{2,0,1:T(1,128)S(1)}, u32[]{:S(2)}, u32[]{:S(2)}) async-start(f32[1,128,256]{2,0,1:T(1,128)} %copy.94), calls=%async_computation | async-start | bytes 262144 | tf_op jit(solution)/shard_map/all_to_all | solution.py:20
  45.7 40.8 %all-to-all-start.1 = ((f32[1,128,1024]{2,0,1:T(1,128)}), f32[1,128,1024]{2,0,1:T(1,128)S(1)}, u32[]{:S(2)}, u32[]{:S(2)}) async-start(f32[1,128,1024]{2,0,1:T(1,128)} %copy.96), calls=%async_computation.1 | async-start | bytes 1048576 | tf_op jit(solution)/shard_map/all_to_all | solution.py:19
  52.9 68.1 %all-gather.3.cloned.1.call-start = ((), (), s32[]{:S(2)}) async-start(), calls=%async_computation.2 | async-start | bytes 2621440 | tf_op jit(solution)/shard_map/all_gather | solution.py:52
  54.8 34.0 %copy-start = (s32[1,32]{1,0:T(1,128)S(1)}, s32[1,32]{1,0:T(1,128)}, u32[]{:S(2)}) copy-start(s32[1,32]{1,0:T(1,128)} %param.14) | copy-start | bytes 388
  122.7 3.8 collective-permute-start
  145.0 12.3 %collective-permute-start.1 = (f32[1024,128]{0,1:T(8,128)S(1)}, f32[1024,128]{0,1:T(8,128)S(1)}, u32[]{:S(2)}, u32[]{:S(2)}) collective-permute-start(f32[1024,128]{0,1:T(8,128)S(1)} %all_gather.26), channel_id=1, source_target_pairs={{0,8},{4,12},{8,0},{12,4},{16,24},{20,28},{24,16},{28,20},{32,40},... | collective-permute-start | bytes 1572872 | tf_op jit(solution)/shard_map/ppermute | solution.py:12
  175.9 21.3 %collective-permute-start.2 = (f32[1024,128]{0,1:T(8,128)S(1)}, f32[1024,128]{0,1:T(8,128)S(1)}, u32[]{:S(2)}, u32[]{:S(2)}) collective-permute-start(f32[1024,128]{0,1:T(8,128)S(1)} %all_gather.27), channel_id=1, source_target_pairs={{0,16},{4,20},{8,24},{12,28},{16,0},{20,4},{24,8},{28,12},{32,48},... | collective-permute-start | bytes 1572872 | tf_op jit(solution)/shard_map/ppermute | solution.py:12
  215.8 47.3 %collective-permute-start.3 = (f32[1024,128]{0,1:T(8,128)S(1)}, f32[1024,128]{0,1:T(8,128)S(1)}, u32[]{:S(2)}, u32[]{:S(2)}) collective-permute-start(f32[1024,128]{0,1:T(8,128)S(1)} %all_gather.28), channel_id=1, source_target_pairs={{0,32},{4,36},{8,40},{12,44},{16,48},{20,52},{24,56},{28,60},{32,0... | collective-permute-start | bytes 1572872 | tf_op jit(solution)/shard_map/ppermute | solution.py:12
  281.8 47.7 %collective-permute-start.4 = (f32[1024,128]{0,1:T(8,128)S(1)}, f32[1024,128]{0,1:T(8,128)S(1)}, u32[]{:S(2)}, u32[]{:S(2)}) collective-permute-start(f32[1024,128]{0,1:T(8,128)S(1)} %all_gather.29), channel_id=1, source_target_pairs={{0,64},{4,68},{8,72},{12,76},{16,80},{20,84},{24,88},{28,92},{32,9... | collective-permute-start | bytes 1572872 | tf_op jit(solution)/shard_map/ppermute | solution.py:12
  347.8 12.7 %collective-permute-start.5 = (f32[1024,128]{0,1:T(8,128)S(1)}, f32[1024,128]{0,1:T(8,128)S(1)}, u32[]{:S(2)}, u32[]{:S(2)}) collective-permute-start(f32[1024,128]{0,1:T(8,128)S(1)} %all_gather.30), channel_id=1, source_target_pairs={{0,128},{4,132},{8,136},{12,140},{16,144},{20,148},{24,152},{28,15... | collective-permute-start | bytes 1572872 | tf_op jit(solution)/shard_map/ppermute | solution.py:12
  379.3 12.6 %collective-permute-start.6 = (f32[1024,128]{0,1:T(8,128)S(1)}, f32[1024,128]{0,1:T(8,128)S(1)}, u32[]{:S(2)}, u32[]{:S(2)}) collective-permute-start(f32[1024,128]{0,1:T(8,128)S(1)} %all_gather.31), channel_id=1, source_target_pairs={{0,256},{4,260},{8,264},{12,268},{16,272},{20,276},{24,280},{28,28... | collective-permute-start | bytes 1572872 | tf_op jit(solution)/shard_map/ppermute | solution.py:12
Sparse Core Ops, SparseCore 0:
  90.9 29.9 all-gather.2
